TPU v7x, 512 devices: a whole 4x8x8 slice. The times are simulated.
512 devices in a mesh: head: 8 (over y), blk: 64 (over z, x, core).
Axes of the slice: x: 4, y: 8, z: 8, core: 2. Of those that a mesh axis runs over, the one named last changes fastest.
Arguments:
- inputs: bfloat16 [4, 64, 7168], P(None, None, 'blk'), may hold values from -40 to 40
- ln_gain: bfloat16 [7168], P('blk'), may hold values from 0.099609375 to 1.8984375
- ln_bias: bfloat16 [7168], P('blk'), may hold values from -3 to 3
- w_query: bfloat16 [7168, 7168], P('blk', 'head'), may hold values from -0.0625 to 0.0625
- w_key: bfloat16 [7168, 7168], P('blk', 'head'), may hold values from -0.0625 to 0.0625
- w_value: bfloat16 [7168, 7168], P('blk', 'head'), may hold values from -0.0625 to 0.0625
- b_query: bfloat16 [7168], P('head'), may hold values from -3 to 3
- b_key: bfloat16 [7168], P('head'), may hold values from -4 to 4
- b_value: bfloat16 [7168], P('head'), may hold values from -3 to 3
- w_out: bfloat16 [7168, 7168], P('head', 'blk'), may hold values from -0.5 to 0.5
- b_out: bfloat16 [7168], P('blk'), may hold values from -3 to 3
- prefix_keys: bfloat16 [1536, 16, 7168], P('blk', None, 'head'), may hold values from -110 to 110
- prefix_values: bfloat16 [1536, 16, 7168], P('blk', None, 'head'), may hold values from -6 to 6
- suffix_keys: bfloat16 [64, 256, 7168], P('blk', None, 'head'), may hold values from -110 to 110
- suffix_values: bfloat16 [64, 256, 7168], P('blk', None, 'head'), may hold values from -6 to 6
- page_table: int32 [8, 288], replicated, may hold values from 0 to 1535, as said below
- prompt_len: int32 [8], replicated, may hold values from 1 to 4608, as said below
- gen_len: int32 [8], replicated, may hold values from 1 to 252, as said below
- parents: int32 [4, 64], replicated, may hold values from 0 to 63, as said below
Outputs:
- hidden: bfloat16 [4, 64, 7168], P(None, None, 'blk')
- final_keys: bfloat16 [64, 256, 7168], P('blk', None, 'head')
- final_values: bfloat16 [64, 256, 7168], P('blk', None, 'head')
Inputs may be any that keep to these rules, and one draw needn't show every extreme that they name: `page_table`: the first ceil(prompt_len[r] / 16) entries of row r are distinct pages that no other request lists; later entries are 0 and hold no tokens of r. `prompt_len`: the longest request has exactly 4608 tokens. `gen_len`: some request has exactly 252. parents[s, b] is a beam of the same request as b.
All inputs are finite; a program needn't handle non-finite values.
Results may differ from a plain program's by a relative error of at most 0.0065.
The roundings to bfloat16 on the way count: a program that leaves them out, or rounds other values in their place, can miss the bound.
Values may be sent and summed in bfloat16 or wider, within the bound.
No kernel may reach another device: no remote copies, remote signals or barrier semaphores. Data moves between devices by JAX's collectives and lax.ppermute only.
A program may use at most 128 MiB of HBM per device.

v0:
```python
import math
import jax
import jax.numpy as jnp
import numpy as np
from jax import lax
from jax.sharding import Mesh
from jax.sharding import PartitionSpec as P

D = 7168
HEAD_DIM = 128
BEAMS = 8
PAGE = 16
GEN = 256
STEPS = 4
MASKED = -1e30
NORM_EPSILON = 1e-05
BLK_PARTS = ("z", "x", "core")
GROUP = ("x", "core")


def nested(reduce, value):
    for axis in reversed(BLK_PARTS):
        value = reduce(value, axis)
    return value


def blk_index():
    index = lax.axis_index("z")
    for axis in BLK_PARTS[1:]:
        index = index * lax.axis_size(axis) + lax.axis_index(axis)
    return index


def body(
    inputs,
    ln_gain,
    ln_bias,
    w_query,
    w_key,
    w_value,
    b_query,
    b_key,
    b_value,
    w_out,
    b_out,
    prefix_keys,
    prefix_values,
    suffix_keys,
    suffix_values,
    page_table,
    prompt_len,
    gen_len,
    parents,
):
    blocks = 1
    for axis in BLK_PARTS:
        blocks *= lax.axis_size(axis)
    me = blk_index()
    steps = inputs.shape[0]
    batch = inputs.shape[1]
    feat_here = w_query.shape[1]
    heads_here = feat_here // HEAD_DIM
    pages_here = prefix_keys.shape[0]
    requests = page_table.shape[0]
    slot_count = page_table.shape[1]
    rows = steps * batch
    score_scale = 1.0 / math.sqrt(HEAD_DIM)
    my_request = me // BEAMS
    first_beam = my_request * BEAMS
    my_gen = gen_len[my_request]
    beam_ids = jnp.arange(batch, dtype=jnp.int32)
    anc = {}
    for s in range(steps):
        x = beam_ids
        anc[s, s] = x
        for t in range(s, -1, -1):
            x = jnp.take(parents[t], x)
            anc[t - 1, s] = x
    origin = jnp.stack([anc[-1, s] for s in range(steps)])
    rows_in = inputs.astype(jnp.float32).reshape(rows, -1)
    stats = jnp.stack([jnp.sum(rows_in, axis=1), jnp.sum(rows_in * rows_in, axis=1)], axis=1)
    stats = nested(lax.psum, stats)
    row_mean = stats[:, 0] / D
    variance = stats[:, 1] / D - row_mean * row_mean
    normed = (
        (rows_in - row_mean[:, None])
        * lax.rsqrt(variance + NORM_EPSILON)[:, None]
        * ln_gain.astype(jnp.float32)
        + ln_bias.astype(jnp.float32)
    ).astype(jnp.bfloat16)
    weights_all = jnp.concatenate([w_query, w_key, w_value], axis=1)
    bias_all = jnp.concatenate([b_query, b_key, b_value]).astype(jnp.float32)
    partial = jnp.dot(normed, weights_all, preferred_element_type=jnp.float32)
    projected = (nested(lax.psum, partial) + bias_all[None, :]).astype(jnp.bfloat16)
    queries = projected[:, :feat_here].reshape(steps, batch, heads_here, HEAD_DIM)
    key_new = projected[:, feat_here : 2 * feat_here].reshape(steps, batch, feat_here)
    value_new = projected[:, 2 * feat_here :].reshape(steps, batch, feat_here)
    beam_request = beam_ids // BEAMS
    beam_prompt = jnp.take(prompt_len, beam_request)
    page_ids = me * pages_here + jnp.arange(pages_here, dtype=jnp.int32)
    slot_ids = jnp.arange(slot_count, dtype=jnp.int32)
    slot_live = slot_ids[None, :] * PAGE < prompt_len[:, None]
    page_match = (
        (page_table[:, :, None] == page_ids[None, None, :]) & slot_live[:, :, None]
    ).astype(jnp.int32)
    request_ids = jnp.arange(requests, dtype=jnp.int32)
    page_request = jnp.sum(page_match * request_ids[:, None, None], axis=(0, 1))
    page_slot = jnp.sum(page_match * slot_ids[None, :, None], axis=(0, 1))
    page_used = jnp.sum(page_match, axis=(0, 1)) > 0
    token_pos = (page_slot[:, None] * PAGE + jnp.arange(PAGE, dtype=jnp.int32)[None, :]).reshape(-1)
    token_request = jnp.repeat(page_request, PAGE)
    token_used = jnp.repeat(page_used, PAGE)
    prefix_live = (
        token_used[None, :]
        & (token_request[None, :] == beam_request[:, None])
        & (token_pos[None, :] < beam_prompt[:, None])
    )
    page_keys = prefix_keys.reshape(pages_here * PAGE, heads_here, HEAD_DIM)
    page_values = prefix_values.reshape(pages_here * PAGE, heads_here, HEAD_DIM)
    flat_queries = queries.reshape(rows, heads_here, HEAD_DIM)
    prompt_scores = (
        jnp.einsum("rhd,thd->rht", flat_queries, page_keys, preferred_element_type=jnp.float32)
        * score_scale
    ).reshape(steps, batch, heads_here, -1)
    prompt_live = prefix_live[None, :, None, :]
    prompt_top = jnp.max(jnp.where(prompt_live, prompt_scores, MASKED), axis=3)
    group_queries = lax.dynamic_slice_in_dim(queries, first_beam, BEAMS, axis=1)
    group_origin = lax.dynamic_slice_in_dim(origin, first_beam, BEAMS, axis=1)
    own_keys = suffix_keys[0].reshape(GEN, heads_here, HEAD_DIM)
    own_values = suffix_values[0].reshape(GEN, heads_here, HEAD_DIM)
    cache_scores = (
        jnp.einsum("sbhd,jhd->sbhj", group_queries, own_keys, preferred_element_type=jnp.float32)
        * score_scale
    )
    gen_rows = jnp.arange(GEN, dtype=jnp.int32)
    cache_live = (group_origin == me)[:, :, None, None] & (gen_rows < my_gen)[None, None, None, :]
    cache_top = jnp.max(jnp.where(cache_live, cache_scores, MASKED), axis=3)
    own_beam = me
    own_queries = lax.dynamic_index_in_dim(queries, own_beam, axis=1, keepdims=False)
    new_src = jnp.stack(
        [
            jnp.stack([anc[t, s][own_beam] if t <= s else own_beam for t in range(steps)])
            for s in range(steps)
        ]
    )
    step_ids = jnp.arange(steps, dtype=jnp.int32)
    new_keys_here = key_new[step_ids[None, :], new_src].reshape(steps, steps, heads_here, HEAD_DIM)
    new_values_here = value_new[step_ids[None, :], new_src].reshape(
        steps, steps, heads_here, HEAD_DIM
    )
    new_scores = (
        jnp.einsum("shd,sthd->sht", own_queries, new_keys_here, preferred_element_type=jnp.float32)
        * score_scale
    )
    new_live = (step_ids[None, :] <= step_ids[:, None])[:, None, :]
    new_top = jnp.max(jnp.where(new_live, new_scores, MASKED), axis=2)
    local_top = prompt_top
    group_top = jnp.maximum(
        lax.dynamic_slice_in_dim(local_top, first_beam, BEAMS, axis=1), cache_top
    )
    local_top = lax.dynamic_update_slice_in_dim(local_top, group_top, first_beam, axis=1)
    own_top = jnp.maximum(
        lax.dynamic_index_in_dim(local_top, own_beam, axis=1, keepdims=True), new_top[:, None]
    )
    local_top = lax.dynamic_update_slice_in_dim(local_top, own_top, own_beam, axis=1)
    top = nested(lax.pmax, local_top)
    prompt_weights = jnp.where(
        prompt_live, jnp.exp(prompt_scores - top[:, :, :, None]), 0.0
    ).astype(jnp.bfloat16)
    weighted = jnp.einsum(
        "rht,thd->rhd",
        prompt_weights.reshape(rows, heads_here, -1),
        page_values,
        preferred_element_type=jnp.float32,
    ).reshape(steps, batch, heads_here, HEAD_DIM)
    totals = jnp.sum(prompt_weights.astype(jnp.float32), axis=3)
    group_top_all = lax.dynamic_slice_in_dim(top, first_beam, BEAMS, axis=1)
    cache_weights = jnp.where(
        cache_live, jnp.exp(cache_scores - group_top_all[:, :, :, None]), 0.0
    ).astype(jnp.bfloat16)
    cache_weighted = jnp.einsum(
        "sbhj,jhd->sbhd", cache_weights, own_values, preferred_element_type=jnp.float32
    )
    cache_totals = jnp.sum(cache_weights.astype(jnp.float32), axis=3)
    own_top_all = lax.dynamic_index_in_dim(top, own_beam, axis=1, keepdims=False)
    new_weights = jnp.where(new_live, jnp.exp(new_scores - own_top_all[:, :, None]), 0.0).astype(
        jnp.bfloat16
    )
    new_weighted = jnp.einsum(
        "sht,sthd->shd", new_weights, new_values_here, preferred_element_type=jnp.float32
    )
    new_totals = jnp.sum(new_weights.astype(jnp.float32), axis=2)
    group_weighted = lax.dynamic_slice_in_dim(weighted, first_beam, BEAMS, axis=1) + cache_weighted
    weighted = lax.dynamic_update_slice_in_dim(weighted, group_weighted, first_beam, axis=1)
    group_totals = lax.dynamic_slice_in_dim(totals, first_beam, BEAMS, axis=1) + cache_totals
    totals = lax.dynamic_update_slice_in_dim(totals, group_totals, first_beam, axis=1)
    own_weighted = (
        lax.dynamic_index_in_dim(weighted, own_beam, axis=1, keepdims=True) + new_weighted[:, None]
    )
    weighted = lax.dynamic_update_slice_in_dim(weighted, own_weighted, own_beam, axis=1)
    own_totals = (
        lax.dynamic_index_in_dim(totals, own_beam, axis=1, keepdims=True) + new_totals[:, None]
    )
    totals = lax.dynamic_update_slice_in_dim(totals, own_totals, own_beam, axis=1)
    lanes = 128
    packed = jnp.concatenate(
        [
            weighted.reshape(rows, feat_here),
            jnp.pad(totals.reshape(rows, heads_here), ((0, 0), (0, lanes - heads_here))),
        ],
        axis=1,
    )
    packed = nested(lax.psum, packed)
    weighted = packed[:, :feat_here].reshape(rows, heads_here, HEAD_DIM)
    totals = packed[:, feat_here : feat_here + heads_here]
    attention = (weighted / totals[:, :, None]).reshape(rows, feat_here).astype(jnp.bfloat16)
    head_terms = jnp.dot(attention, w_out, preferred_element_type=jnp.float32)
    head_total = lax.psum(head_terms, "head")
    hidden = (head_total + b_out.astype(jnp.float32)[None, :]).astype(jnp.bfloat16)
    hidden = hidden.reshape(steps, batch, -1)
    final_origin = origin[steps - 1]
    pick = lax.dynamic_slice_in_dim(final_origin, first_beam, BEAMS) - first_beam
    my_final_src = [anc[t, steps - 1][own_beam] for t in range(steps)]
    write_rows = my_gen + step_ids

    def reorder(cache, fresh):
        chunks = cache[0].reshape(BEAMS, GEN // BEAMS, feat_here)
        spread = lax.all_to_all(chunks, GROUP, 0, 0, tiled=True)
        picked = jnp.take(spread, pick, axis=0)
        back = lax.all_to_all(picked, GROUP, 0, 0, tiled=True).reshape(GEN, feat_here)
        new_rows = jnp.stack([fresh[t, my_final_src[t]] for t in range(steps)])
        hit = gen_rows[:, None] == write_rows[None, :]
        chosen = jnp.argmax(hit, axis=1)
        out = jnp.where(jnp.any(hit, axis=1)[:, None], jnp.take(new_rows, chosen, axis=0), back)
        return out[None]

    final_keys = reorder(suffix_keys, key_new)
    final_values = reorder(suffix_values, value_new)
    return (hidden, final_keys, final_values)


def solution(mesh):
    heads = mesh.shape["head"]
    blocks = mesh.shape["blk"]
    cores = 2
    group_chips = BEAMS // cores
    devices = np.asarray(mesh.devices).reshape(heads, blocks // BEAMS, group_chips, cores)
    fine = Mesh(devices, ("head",) + BLK_PARTS)
    blk = BLK_PARTS
    in_specs = (
        P(None, None, blk),
        P(blk),
        P(blk),
        P(blk, "head"),
        P(blk, "head"),
        P(blk, "head"),
        P("head"),
        P("head"),
        P("head"),
        P("head", blk),
        P(blk),
        P(blk, None, "head"),
        P(blk, None, "head"),
        P(blk, None, "head"),
        P(blk, None, "head"),
        P(),
        P(),
        P(),
        P(),
    )
    out_specs = (P(None, None, blk), P(blk, None, "head"), P(blk, None, "head"))
    return jax.shard_map(body, mesh=fine, in_specs=in_specs, out_specs=out_specs, check_vma=False)
```

profile of v0, /device:TPU:2, one launch (start us, length us, event | category | flops | bytes accessed | tf_op | source)
XLA Modules:
  0.0 610.5 jit_solution(4780817149313871015)
XLA Ops:
  9.7 2.5 psum.70
  12.2 13.6 %psum.71 = f32[256,2]{0,1:T(2,128)S(1)} all-reduce(f32[256,2]{0,1:T(2,128)S(1)} %psum.70), channel_id=1, replica_groups=mesh['head'=8,'z'=8,'x'=4,'core'=2] {'x'}, use_global_device_ids=true, to_apply=%region_6.7 | all-reduce | flops 512 | bytes 4096 | tf_op jit(solution)/shard_map/psum | solution.py:23
  25.8 18.2 %psum.72 = f32[256,2]{0,1:T(2,128)S(1)} all-reduce(f32[256,2]{0,1:T(2,128)S(1)} %psum.71), channel_id=1, replica_groups=mesh['head'=8,'z'=8,'x'=4,'core'=2] {'z'}, use_global_device_ids=true, to_apply=%region_7.8 | all-reduce | flops 512 | bytes 4096 | tf_op jit(solution)/shard_map/psum | solution.py:23
  44.9 3.2 fusion.12
  48.2 35.7 %all-reduce.9.cloned.1.call-done = f32[256,2688]{1,0:T(8,128)} async-done(((f32[256,2688]{1,0:T(8,128)}), f32[256,2688]{1,0:T(8,128)}) %all-reduce.9.cloned.1.call-update) | async-done | bytes 2752528 | tf_op jit(solution)/shard_map/psum | solution.py:23
  92.2 74.5 %all-reduce.11.cloned.1.call-done = f32[256,2688]{1,0:T(8,128)} async-done(((f32[256,2688]{1,0:T(8,128)}), f32[256,2688]{1,0:T(8,128)}) %all-reduce.11.cloned.1.call-update) | async-done | bytes 2752528 | tf_op jit(solution)/shard_map/psum | solution.py:23
  184.5 5.1 and_select_fusion.7
  189.8 73.7 %all-reduce.13.cloned.1.call-done = f32[256,2688]{1,0:T(8,128)} async-done(((f32[256,2688]{1,0:T(8,128)}), f32[256,2688]{1,0:T(8,128)}) %all-reduce.13.cloned.1.call-update) | async-done | bytes 2752528 | tf_op jit(solution)/shard_map/psum | solution.py:23
  268.1 2.1 fusion
  274.7 3.3 pmax.21
  278.0 13.9 %pmax.22 = f32[4,64,7]{1,0,2:T(4,128)S(1)} all-reduce(f32[4,64,7]{1,0,2:T(4,128)S(1)} %pmax.21), channel_id=1, replica_groups=mesh['head'=8,'z'=8,'x'=4,'core'=2] {'x'}, use_global_device_ids=true, to_apply=%region_15.17 | all-reduce | flops 1792 | bytes 14336 | tf_op jit(solution)/shard_map/pmax | solution.py:23
  291.9 30.1 %pmax.23 = f32[4,64,7]{1,0,2:T(4,128)S(1)} all-reduce(f32[4,64,7]{1,0,2:T(4,128)S(1)} %pmax.22), channel_id=1, replica_groups=mesh['head'=8,'z'=8,'x'=4,'core'=2] {'z'}, use_global_device_ids=true, to_apply=%region_16.18 | all-reduce | flops 1792 | bytes 14336 | tf_op jit(solution)/shard_map/pmax | solution.py:23
  325.1 2.9 fusion.8
  330.1 2.0 fusion.6
  337.7 36.2 %all-reduce.15.cloned.1.call-done = f32[256,1024]{1,0:T(8,128)} async-done(((f32[256,1024]{1,0:T(8,128)}), f32[256,1024]{1,0:T(8,128)}) %all-reduce.15.cloned.1.call-update) | async-done | bytes 1048592 | tf_op jit(solution)/shard_map/psum | solution.py:23
  374.0 4.9 all-to-all-start.2
  387.1 4.8 all-to-all-start
  392.0 44.4 %all-reduce.17.cloned.1.call-done = f32[256,1024]{1,0:T(8,128)} async-done(((f32[256,1024]{1,0:T(8,128)}), f32[256,1024]{1,0:T(8,128)}) %all-reduce.17.cloned.1.call-update) | async-done | bytes 1048592 | tf_op jit(solution)/shard_map/psum | solution.py:23
  438.8 4.8 all-to-all-start.3
  445.2 6.6 %all-to-all-done.3 = bf16[8,32,896]{2,1,0:T(8,128)(2,1)S(1)} async-done(((bf16[8,32,896]{2,1,0:T(8,128)(2,1)}), bf16[8,32,896]{2,1,0:T(8,128)(2,1)S(1)}, u32[]{:S(2)}, u32[]{:S(2)}) %all-to-all-start.3) | async-done | bytes 458784 | tf_op jit(solution)/shard_map/all_to_all | solution.py:230
  451.8 4.8 all-to-all-start.1
  459.1 63.0 %all-reduce.19.cloned.1.call-done = f32[256,1024]{1,0:T(8,128)} async-done(((f32[256,1024]{1,0:T(8,128)}), f32[256,1024]{1,0:T(8,128)}) %all-reduce.19.cloned.1.call-update) | async-done | bytes 1048592 | tf_op jit(solution)/shard_map/psum | solution.py:23
  524.4 2.4 fusion.18
  528.1 73.9 %all-reduce.21.cloned.1.call-done = f32[256,112]{0,1:T(8,128)} async-done(((f32[256,112]{0,1:T(8,128)}), f32[256,112]{0,1:T(8,128)}) %all-reduce.21.cloned.1.call-update) | async-done | bytes 114704 | tf_op jit(solution)/shard_map/psum | solution.py:218
  (178 shorter events, 63.9 us)
Async XLA Ops:
  7.2 517.2 %copy-start = (bf16[896,112]{0,1:T(8,128)(2,1)S(1)}, bf16[896,112]{0,1:T(8,128)(2,1)}, u32[]{:S(2)}) copy-start(bf16[896,112]{0,1:T(8,128)(2,1)} %param.34) | copy-start | bytes 602116
  7.2 76.7 %all-reduce.9.cloned.1.call-start = ((), (), s32[]{:S(2)}) async-start(), calls=%async_computation.4 | async-start | bytes 5505024 | tf_op jit(solution)/shard_map/psum | solution.py:23
  48.1 35.9 %copy-start.3 = (s32[8]{0:T(128)S(1)}, s32[8]{0:T(128)}, u32[]{:S(2)}) copy-start(s32[8]{0:T(128)} %param.41) | copy-start | bytes 100
  48.1 36.0 %copy-start.4 = (s32[8,288]{1,0:T(8,128)S(1)}, s32[8,288]{1,0:T(8,128)}, u32[]{:S(2)}) copy-start(s32[8,288]{1,0:T(8,128)} %param.40) | copy-start | bytes 27652
  48.1 36.8 %copy-start.1 = (bf16[24,16,896]{2,1,0:T(8,128)(2,1)S(1)}, bf16[24,16,896]{2,1,0:T(8,128)(2,1)}, u32[]{:S(2)}) copy-start(bf16[24,16,896]{2,1,0:T(8,128)(2,1)} %param.36) | copy-start | bytes 2064388
  48.2 38.5 %copy-start.8 = (s32[4,64]{1,0:T(4,128)S(1)}, s32[4,64]{1,0:T(4,128)}, u32[]{:S(2)}) copy-start(s32[4,64]{1,0:T(4,128)} %param.43) | copy-start | bytes 3076
  48.2 118.5 %all-reduce.11.cloned.1.call-start = ((), (), s32[]{:S(2)}) async-start(), calls=%async_computation.5 | async-start | bytes 5505024 | tf_op jit(solution)/shard_map/psum | solution.py:23
  83.9 179.6 %all-reduce.13.cloned.1.call-start = ((), (), s32[]{:S(2)}) async-start(), calls=%async_computation.6 | async-start | bytes 5505024 | tf_op jit(solution)/shard_map/psum | solution.py:23
  92.2 86.5 %copy-start.2 = (bf16[24,16,896]{2,1,0:T(8,128)(2,1)S(1)}, bf16[24,16,896]{2,1,0:T(8,128)(2,1)}, u32[]{:S(2)}) copy-start(bf16[24,16,896]{2,1,0:T(8,128)(2,1)} %param.37) | copy-start | bytes 2064388
  166.7 15.6 %copy-start.9 = (s32[8]{0:T(128)S(1)}, s32[8]{0:T(128)}, u32[]{:S(2)}) copy-start(s32[8]{0:T(128)} %param.42) | copy-start | bytes 100
  166.7 22.8 %copy-start.5 = (bf16[896]{0:T(1024)(128)(2,1)S(1)}, bf16[896]{0:T(1024)(128)(2,1)}, u32[]{:S(2)}) copy-start(bf16[896]{0:T(1024)(128)(2,1)} %param.33) | copy-start | bytes 5380
  166.7 22.8 %copy-start.6 = (bf16[896]{0:T(1024)(128)(2,1)S(1)}, bf16[896]{0:T(1024)(128)(2,1)}, u32[]{:S(2)}) copy-start(bf16[896]{0:T(1024)(128)(2,1)} %param.32) | copy-start | bytes 5380
  166.7 22.8 %copy-start.7 = (bf16[896]{0:T(1024)(128)(2,1)S(1)}, bf16[896]{0:T(1024)(128)(2,1)}, u32[]{:S(2)}) copy-start(bf16[896]{0:T(1024)(128)(2,1)} %param.31) | copy-start | bytes 5380
  166.7 207.2 %all-reduce.15.cloned.1.call-start = ((), (), s32[]{:S(2)}) async-start(), calls=%async_computation.7 | async-start | bytes 2097152 | tf_op jit(solution)/shard_map/psum | solution.py:23
  336.5 46.0 %copy-start.10 = (bf16[112]{0:T(256)(128)(2,1)S(1)}, bf16[112]{0:T(256)(128)(2,1)}, u32[]{:S(2)}) copy-start(bf16[112]{0:T(256)(128)(2,1)} %param.35) | copy-start | bytes 676
  337.7 98.7 %all-reduce.17.cloned.1.call-start = ((), (), s32[]{:S(2)}) async-start(), calls=%async_computation.8 | async-start | bytes 2097152 | tf_op jit(solution)/shard_map/psum | solution.py:23
  374.0 13.2 %all-to-all-start.2 = ((bf16[8,32,896]{2,1,0:T(8,128)(2,1)}), bf16[8,32,896]{2,1,0:T(8,128)(2,1)S(1)}, u32[]{:S(2)}, u32[]{:S(2)}) async-start(bf16[8,32,896]{2,1,0:T(8,128)(2,1)} %bitcast.68), calls=%async_computation.2 | async-start | bytes 917504 | tf_op jit(solution)/shard_map/all_to_all | solution.py:228
  387.1 49.9 %all-to-all-start = ((bf16[8,32,896]{2,1,0:T(8,128)(2,1)}), bf16[8,32,896]{2,1,0:T(8,128)(2,1)S(1)}, u32[]{:S(2)}, u32[]{:S(2)}) async-start(bf16[8,32,896]{2,1,0:T(8,128)(2,1)} %bitcast.61), calls=%async_computation | async-start | bytes 917504 | tf_op jit(solution)/shard_map/all_to_all | solution.py:228
  392.0 130.1 %all-reduce.19.cloned.1.call-start = ((), (), s32[]{:S(2)}) async-start(), calls=%async_computation.9 | async-start | bytes 2097152 | tf_op jit(solution)/shard_map/psum | solution.py:23
  438.8 13.0 %all-to-all-start.3 = ((bf16[8,32,896]{2,1,0:T(8,128)(2,1)}), bf16[8,32,896]{2,1,0:T(8,128)(2,1)S(1)}, u32[]{:S(2)}, u32[]{:S(2)}) async-start(bf16[8,32,896]{2,1,0:T(8,128)(2,1)} %get-tuple-element.45), calls=%async_computation.3 | async-start | bytes 917504 | tf_op jit(solution)/shard_map/all_to_all | solution.py:230
  451.8 75.1 %all-to-all-start.1 = ((bf16[8,32,896]{2,1,0:T(8,128)(2,1)}), bf16[8,32,896]{2,1,0:T(8,128)(2,1)S(1)}, u32[]{:S(2)}, u32[]{:S(2)}) async-start(bf16[8,32,896]{2,1,0:T(8,128)(2,1)} %get-tuple-element.46), calls=%async_computation.1 | async-start | bytes 917504 | tf_op jit(solution)/shard_map/all_to_all | solution.py:230
  456.6 145.4 %all-reduce.21.cloned.1.call-start = ((), (), s32[]{:S(2)}) async-start(), calls=%async_computation.10 | async-start | bytes 229376 | tf_op jit(solution)/shard_map/psum | solution.py:218
Sparse Core Ops, SparseCore 0:
  48.3 35.5 all-reduce.8
  86.4 80.2 all-reduce.10
  169.2 94.2 all-reduce.12
  337.8 36.1 all-reduce.14
  376.3 60.0 all-reduce.16
  438.6 83.4 all-reduce.18
  527.0 74.9 all-reduce.20
where the time goes:
time: 612 us; the launch traced here: 611 us
  waiting for transfers between devices  409 us (67%)
  blocking collectives  81.5 us (13%)
  local copies, waits for them, and re-layouts  41.3 us (7%)
  other arithmetic  24.4 us (4%)
  between operations  20.1 us (3%)
  starting transfers between devices  19.6 us (3%)
  matrix products  14.2 us (2%)
    psum x6, waiting for transfers between devices, nested(): value = reduce(value, axis)  328 us
    psum x1, waiting for transfers between devices, body(): head_total = lax.psum(head_terms, 'head')  73.9 us
    pmax x3, blocking collectives, nested(): value = reduce(value, axis)  47.3 us
    psum x3, blocking collectives, nested(): value = reduce(value, axis)  34.2 us
  transfers between devices with their start and end apart: 11, of which 9 were waited for; matrix products, arithmetic and copies ran while one was open for 7% of the time, Pallas kernels for 0%

commit v1 on v0

--- a/solution.py
+++ b/solution.py
@@ -215,7 +215,8 @@
     totals = packed[:, feat_here : feat_here + heads_here]
     attention = (weighted / totals[:, :, None]).reshape(rows, feat_here).astype(jnp.bfloat16)
     head_terms = jnp.dot(attention, w_out, preferred_element_type=jnp.float32)
-    head_total = lax.psum(head_terms, "head")
+    answer = lax.all_gather(head_terms, axis_name="head")
+    head_total = jnp.sum(answer, axis=0)
     hidden = (head_total + b_out.astype(jnp.float32)[None, :]).astype(jnp.bfloat16)
     hidden = hidden.reshape(steps, batch, -1)
     final_origin = origin[steps - 1]

time: 612 us -> 561 us (0.917)
  waiting for transfers between devices: 409 us -> 332 us
  blocking collectives: 81.5 us -> 109 us
    psum x1 -> x0, waiting for transfers between devices: 73.9 us -> none  [body(): head_total = lax.psum(head_terms, 'head')]
    all_gather x0 -> x1, blocking collectives: none -> 27.5 us  [body(): answer = lax.all_gather(head_terms, axis_name='head')]
    psum x6, waiting for transfers between devices: 328 us -> 321 us  [nested(): value = reduce(value, axis)]
  transfers between devices with their start and end apart: 11 -> 10, of which waited for: 9 -> 8; matrix products, arithmetic and copies ran while one was open for 7% -> 7% of each run, Pallas kernels for 0% -> 0%
where the time goes in v1:
time: 561 us; the launch traced here: 560 us
  waiting for transfers between devices  332 us (59%)
  blocking collectives  109 us (19%)
  local copies, waits for them, and re-layouts  40.2 us (7%)
  other arithmetic  24.4 us (4%)
  starting transfers between devices  21.1 us (4%)
  between operations  20.3 us (4%)
  matrix products  12.1 us (2%)
    psum x6, waiting for transfers between devices, nested(): value = reduce(value, axis)  321 us
    pmax x3, blocking collectives, nested(): value = reduce(value, axis)  47.3 us
    psum x3, blocking collectives, nested(): value = reduce(value, axis)  34.2 us
    all_gather x1, blocking collectives, body(): answer = lax.all_gather(head_terms, axis_name='head')  27.5 us
    all_to_all x2, starting transfers between devices, reorder(): spread = lax.all_to_all(chunks, GROUP, 0, 0, tiled=True)  11.4 us
  transfers between devices with their start and end apart: 10, of which 8 were waited for; matrix products, arithmetic and copies ran while one was open for 7% of the time, Pallas kernels for 0%

profile of v1, /device:TPU:2, one launch (start us, length us, event | category | flops | bytes accessed | tf_op | source)
XLA Modules:
  0.0 559.5 jit_solution(11922454372975548873)
XLA Ops:
  9.7 2.5 psum.63
  12.2 13.6 %psum.64 = f32[256,2]{0,1:T(2,128)S(1)} all-reduce(f32[256,2]{0,1:T(2,128)S(1)} %psum.63), channel_id=1, replica_groups=mesh['head'=8,'z'=8,'x'=4,'core'=2] {'x'}, use_global_device_ids=true, to_apply=%region_6.7 | all-reduce | flops 512 | bytes 4096 | tf_op jit(solution)/shard_map/psum | solution.py:23
  25.8 18.2 %psum.65 = f32[256,2]{0,1:T(2,128)S(1)} all-reduce(f32[256,2]{0,1:T(2,128)S(1)} %psum.64), channel_id=1, replica_groups=mesh['head'=8,'z'=8,'x'=4,'core'=2] {'z'}, use_global_device_ids=true, to_apply=%region_7.8 | all-reduce | flops 512 | bytes 4096 | tf_op jit(solution)/shard_map/psum | solution.py:23
  44.9 3.2 fusion.12
  48.2 35.7 %all-reduce.8.cloned.1.call-done = f32[256,2688]{1,0:T(8,128)} async-done(((f32[256,2688]{1,0:T(8,128)}), f32[256,2688]{1,0:T(8,128)}) %all-reduce.8.cloned.1.call-update) | async-done | bytes 2752528 | tf_op jit(solution)/shard_map/psum | solution.py:23
  92.2 74.5 %all-reduce.10.cloned.1.call-done = f32[256,2688]{1,0:T(8,128)} async-done(((f32[256,2688]{1,0:T(8,128)}), f32[256,2688]{1,0:T(8,128)}) %all-reduce.10.cloned.1.call-update) | async-done | bytes 2752528 | tf_op jit(solution)/shard_map/psum | solution.py:23
  184.6 5.1 and_select_fusion.7
  190.0 73.6 %all-reduce.12.cloned.1.call-done = f32[256,2688]{1,0:T(8,128)} async-done(((f32[256,2688]{1,0:T(8,128)}), f32[256,2688]{1,0:T(8,128)}) %all-reduce.12.cloned.1.call-update) | async-done | bytes 2752528 | tf_op jit(solution)/shard_map/psum | solution.py:23
  268.1 2.1 fusion
  274.7 3.3 pmax.21
  278.0 13.9 %pmax.22 = f32[4,64,7]{1,0,2:T(4,128)S(1)} all-reduce(f32[4,64,7]{1,0,2:T(4,128)S(1)} %pmax.21), channel_id=1, replica_groups=mesh['head'=8,'z'=8,'x'=4,'core'=2] {'x'}, use_global_device_ids=true, to_apply=%region_15.17 | all-reduce | flops 1792 | bytes 14336 | tf_op jit(solution)/shard_map/pmax | solution.py:23
  291.9 30.1 %pmax.23 = f32[4,64,7]{1,0,2:T(4,128)S(1)} all-reduce(f32[4,64,7]{1,0,2:T(4,128)S(1)} %pmax.22), channel_id=1, replica_groups=mesh['head'=8,'z'=8,'x'=4,'core'=2] {'z'}, use_global_device_ids=true, to_apply=%region_16.18 | all-reduce | flops 1792 | bytes 14336 | tf_op jit(solution)/shard_map/pmax | solution.py:23
  325.1 2.9 fusion.8
  330.1 2.0 fusion.6
  337.7 6.4 %all-to-all-start.2 = ((bf16[8,32,896]{2,1,0:T(8,128)(2,1)}), bf16[8,32,896]{2,1,0:T(8,128)(2,1)S(1)}, u32[]{:S(2)}, u32[]{:S(2)}) async-start(bf16[8,32,896]{2,1,0:T(8,128)(2,1)} %bitcast.68), calls=%async_computation.2 | async-start | bytes 917504 | tf_op jit(solution)/shard_map/all_to_all | solution.py:229
  349.8 24.2 %all-reduce.14.cloned.1.call-done = f32[256,1024]{1,0:T(8,128)} async-done(((f32[256,1024]{1,0:T(8,128)}), f32[256,1024]{1,0:T(8,128)}) %all-reduce.14.cloned.1.call-update) | async-done | bytes 1048592 | tf_op jit(solution)/shard_map/psum | solution.py:23
  374.7 4.9 all-to-all-start
  380.9 7.0 %all-to-all-done = bf16[8,32,896]{2,1,0:T(8,128)(2,1)S(1)} async-done(((bf16[8,32,896]{2,1,0:T(8,128)(2,1)}), bf16[8,32,896]{2,1,0:T(8,128)(2,1)S(1)}, u32[]{:S(2)}, u32[]{:S(2)}) %all-to-all-start) | async-done | bytes 458784 | tf_op jit(solution)/shard_map/all_to_all | solution.py:229
  389.6 4.8 all-to-all-start.3
  394.5 41.9 %all-reduce.16.cloned.1.call-done = f32[256,1024]{1,0:T(8,128)} async-done(((f32[256,1024]{1,0:T(8,128)}), f32[256,1024]{1,0:T(8,128)}) %all-reduce.16.cloned.1.call-update) | async-done | bytes 1048592 | tf_op jit(solution)/shard_map/psum | solution.py:23
  436.4 4.8 all-to-all-start.1
  445.3 4.1 all-to-all-done.1
  450.7 71.4 %all-reduce.18.cloned.1.call-done = f32[256,1024]{1,0:T(8,128)} async-done(((f32[256,1024]{1,0:T(8,128)}), f32[256,1024]{1,0:T(8,128)}) %all-reduce.18.cloned.1.call-update) | async-done | bytes 1048592 | tf_op jit(solution)/shard_map/psum | solution.py:23
  523.9 27.5 %all-gather = f32[2048,112]{0,1:T(8,128)S(1)} all-gather(f32[256,112]{0,1:T(8,128)S(1)} %fusion.18), channel_id=2, replica_groups=mesh['head'=8,'z'=8,'x'=4,'core'=2] {'head'}, dimensions={0}, use_global_device_ids=true | all-gather | bytes 1032192 | tf_op jit(solution)/shard_map/all_gather | solution.py:218
  (180 shorter events, 61.6 us)
Async XLA Ops:
  7.2 516.4 %copy-start = (bf16[896,112]{0,1:T(8,128)(2,1)S(1)}, bf16[896,112]{0,1:T(8,128)(2,1)}, u32[]{:S(2)}) copy-start(bf16[896,112]{0,1:T(8,128)(2,1)} %param.34) | copy-start | bytes 602116
  7.2 76.7 %all-reduce.8.cloned.1.call-start = ((), (), s32[]{:S(2)}) async-start(), calls=%async_computation.4 | async-start | bytes 5505024 | tf_op jit(solution)/shard_map/psum | solution.py:23
  48.1 35.9 %copy-start.3 = (s32[8]{0:T(128)S(1)}, s32[8]{0:T(128)}, u32[]{:S(2)}) copy-start(s32[8]{0:T(128)} %param.41) | copy-start | bytes 100
  48.1 36.0 %copy-start.5 = (s32[8,288]{1,0:T(8,128)S(1)}, s32[8,288]{1,0:T(8,128)}, u32[]{:S(2)}) copy-start(s32[8,288]{1,0:T(8,128)} %param.40) | copy-start | bytes 27652
  48.1 36.8 %copy-start.1 = (bf16[24,16,896]{2,1,0:T(8,128)(2,1)S(1)}, bf16[24,16,896]{2,1,0:T(8,128)(2,1)}, u32[]{:S(2)}) copy-start(bf16[24,16,896]{2,1,0:T(8,128)(2,1)} %param.36) | copy-start | bytes 2064388
  48.2 38.5 %copy-start.9 = (s32[4,64]{1,0:T(4,128)S(1)}, s32[4,64]{1,0:T(4,128)}, u32[]{:S(2)}) copy-start(s32[4,64]{1,0:T(4,128)} %param.43) | copy-start | bytes 3076
  48.2 118.5 %all-reduce.10.cloned.1.call-start = ((), (), s32[]{:S(2)}) async-start(), calls=%async_computation.5 | async-start | bytes 5505024 | tf_op jit(solution)/shard_map/psum | solution.py:23
  83.9 179.6 %all-reduce.12.cloned.1.call-start = ((), (), s32[]{:S(2)}) async-start(), calls=%async_computation.6 | async-start | bytes 5505024 | tf_op jit(solution)/shard_map/psum | solution.py:23
  92.2 86.7 %copy-start.2 = (bf16[24,16,896]{2,1,0:T(8,128)(2,1)S(1)}, bf16[24,16,896]{2,1,0:T(8,128)(2,1)}, u32[]{:S(2)}) copy-start(bf16[24,16,896]{2,1,0:T(8,128)(2,1)} %param.37) | copy-start | bytes 2064388
  166.7 15.8 %copy-start.10 = (s32[8]{0:T(128)S(1)}, s32[8]{0:T(128)}, u32[]{:S(2)}) copy-start(s32[8]{0:T(128)} %param.42) | copy-start | bytes 100
  166.7 23.0 %copy-start.6 = (bf16[896]{0:T(1024)(128)(2,1)S(1)}, bf16[896]{0:T(1024)(128)(2,1)}, u32[]{:S(2)}) copy-start(bf16[896]{0:T(1024)(128)(2,1)} %param.33) | copy-start | bytes 5380
  166.7 23.0 %copy-start.7 = (bf16[896]{0:T(1024)(128)(2,1)S(1)}, bf16[896]{0:T(1024)(128)(2,1)}, u32[]{:S(2)}) copy-start(bf16[896]{0:T(1024)(128)(2,1)} %param.32) | copy-start | bytes 5380
  166.7 23.0 %copy-start.8 = (bf16[896]{0:T(1024)(128)(2,1)S(1)}, bf16[896]{0:T(1024)(128)(2,1)}, u32[]{:S(2)}) copy-start(bf16[896]{0:T(1024)(128)(2,1)} %param.31) | copy-start | bytes 5380
  166.7 207.2 %all-reduce.14.cloned.1.call-start = ((), (), s32[]{:S(2)}) async-start(), calls=%async_computation.7 | async-start | bytes 2097152 | tf_op jit(solution)/shard_map/psum | solution.py:23
  336.3 11.5 %copy-start.11 = (bf16[112]{0:T(256)(128)(2,1)S(1)}, bf16[112]{0:T(256)(128)(2,1)}, u32[]{:S(2)}) copy-start(bf16[112]{0:T(256)(128)(2,1)} %param.35) | copy-start | bytes 676
  337.7 37.0 %all-to-all-start.2 = ((bf16[8,32,896]{2,1,0:T(8,128)(2,1)}), bf16[8,32,896]{2,1,0:T(8,128)(2,1)S(1)}, u32[]{:S(2)}, u32[]{:S(2)}) async-start(bf16[8,32,896]{2,1,0:T(8,128)(2,1)} %bitcast.68), calls=%async_computation.2 | async-start | bytes 917504 | tf_op jit(solution)/shard_map/all_to_all | solution.py:229
  344.1 92.3 %all-reduce.16.cloned.1.call-start = ((), (), s32[]{:S(2)}) async-start(), calls=%async_computation.8 | async-start | bytes 2097152 | tf_op jit(solution)/shard_map/psum | solution.py:23
  374.7 13.2 %all-to-all-start = ((bf16[8,32,896]{2,1,0:T(8,128)(2,1)}), bf16[8,32,896]{2,1,0:T(8,128)(2,1)S(1)}, u32[]{:S(2)}, u32[]{:S(2)}) async-start(bf16[8,32,896]{2,1,0:T(8,128)(2,1)} %bitcast.61), calls=%async_computation | async-start | bytes 917504 | tf_op jit(solution)/shard_map/all_to_all | solution.py:229
  389.6 46.9 %all-to-all-start.3 = ((bf16[8,32,896]{2,1,0:T(8,128)(2,1)}), bf16[8,32,896]{2,1,0:T(8,128)(2,1)S(1)}, u32[]{:S(2)}, u32[]{:S(2)}) async-start(bf16[8,32,896]{2,1,0:T(8,128)(2,1)} %get-tuple-element.42), calls=%async_computation.3 | async-start | bytes 917504 | tf_op jit(solution)/shard_map/all_to_all | solution.py:231
  394.4 127.7 %all-reduce.18.cloned.1.call-start = ((), (), s32[]{:S(2)}) async-start(), calls=%async_computation.9 | async-start | bytes 2097152 | tf_op jit(solution)/shard_map/psum | solution.py:23
  436.4 13.0 %all-to-all-start.1 = ((bf16[8,32,896]{2,1,0:T(8,128)(2,1)}), bf16[8,32,896]{2,1,0:T(8,128)(2,1)S(1)}, u32[]{:S(2)}, u32[]{:S(2)}) async-start(bf16[8,32,896]{2,1,0:T(8,128)(2,1)} %get-tuple-element.43), calls=%async_computation.1 | async-start | bytes 917504 | tf_op jit(solution)/shard_map/all_to_all | solution.py:231
  522.1 1.5 copy-start.4
Sparse Core Ops, SparseCore 0:
  48.3 35.5 all-reduce.7
  86.4 80.2 all-reduce.9
  169.2 94.2 all-reduce.11
  337.8 36.1 all-reduce.13
  376.3 60.0 all-reduce.15
  438.6 83.4 all-reduce.17
